TPU v7x, 128 devices: a whole 4x4x4 slice. The times are simulated.
128 devices in a mesh: node: 4 (over x), ep: 32 (over y, z, core).
Axes of the slice: x: 4, y: 4, z: 4, core: 2. Of those that a mesh axis runs over, the one named last changes fastest.
Arguments:
- images: bfloat16 [128, 257, 1280], P(('node', 'ep')), may hold values from -6 to 6
- w_query: bfloat16 [1280, 1280], P(None, 'node'), may hold values from -6 to 6
- w_key: bfloat16 [1280, 1280], P(None, 'node'), may hold values from -6 to 6
- w_value: bfloat16 [1280, 1280], P(None, 'node'), may hold values from -0.15625 to 0.15625
- w_output: bfloat16 [1280, 1280], replicated, may hold values from -0.15625 to 0.15625
- router: bfloat16 [1280, 32], replicated, may hold values from -0.15625 to 0.15625
- w_in: bfloat16 [32, 1280, 5120], P('ep', None, 'node'), may hold values from -0.15625 to 0.15625
- w_out: bfloat16 [32, 5120, 1280], P('ep', 'node'), may hold values from -0.078125 to 0.078125
- routes: int32 [128, 257, 2], P(('node', 'ep')), may hold values from 0 to 31, all different within a row; in each aligned block of 257 rows (0 to 256, 257 to 513, ..., all dimensions but the last counted through in order) at most 24 rows name the same one
Outputs:
- output: bfloat16 [128, 257, 1280], P(('node', 'ep'))
Inputs may be any that keep to these rules, and one draw needn't show every extreme that they name: `routes`: the two experts of a token differ. At most 24 tokens of one image name the same expert, and in every draw some image has an expert named by exactly 24 of its tokens.
All inputs are finite; a program needn't handle non-finite values.
Results may differ from a plain program's by a relative error of at most 0.0085.
Values may be sent and summed in bfloat16 or wider, within the bound.
No kernel may reach another device: no remote copies, remote signals or barrier semaphores. Data moves between devices by JAX's collectives and lax.ppermute only.
A program may use at most 128 MiB of HBM per device.

v0:
```python
import math
import jax
import jax.numpy as jnp
from jax import lax
from jax.sharding import PartitionSpec as P

D = 1280
HEADS = 16
CAP = 24


def layer_norm(values):
    center = values - jnp.mean(values, axis=-1, keepdims=True)
    spread = jnp.mean(center * center, axis=-1, keepdims=True)
    return center * lax.rsqrt(spread + 1e-06)


def slot_table(chosen, num_experts):
    onehot = (chosen[..., None] == jnp.arange(num_experts, dtype=jnp.int32)).astype(jnp.int32)
    before = jnp.cumsum(onehot, axis=1) - onehot
    return jnp.sum(before * onehot, axis=-1)


def shards(images, w_query, w_key, w_value, w_output, router, w_in, w_out, routes):
    local_images, tokens_dev, width = images.shape
    head_size = D // HEADS
    local_heads = w_query.shape[1] // head_size
    node_count = lax.axis_size("node")
    column_count = lax.axis_size("ep")
    num_experts = router.shape[1]
    local_experts = w_in.shape[0]
    slot_count = local_images * CAP
    inputs = images.astype(jnp.float32)
    normed = layer_norm(inputs).astype(jnp.bfloat16)
    shard_rows = lax.all_gather(normed, "node", axis=0, tiled=True)
    number = shard_rows.shape[0]
    queries = jnp.einsum(
        "ctd,de->cte", shard_rows, w_query, preferred_element_type=jnp.float32
    ).astype(jnp.bfloat16)
    projected_keys = jnp.einsum(
        "ctd,de->cte", shard_rows, w_key, preferred_element_type=jnp.float32
    ).astype(jnp.bfloat16)
    projected_values = jnp.einsum(
        "ctd,de->cte", shard_rows, w_value, preferred_element_type=jnp.float32
    ).astype(jnp.bfloat16)
    query_heads = queries.reshape(number, tokens_dev, local_heads, head_size)
    key_heads = projected_keys.reshape(number, tokens_dev, local_heads, head_size)
    value_heads = projected_values.reshape(number, tokens_dev, local_heads, head_size)
    scores = jnp.einsum(
        "cqhd,ckhd->chqk", query_heads, key_heads, preferred_element_type=jnp.float32
    ) / math.sqrt(head_size)
    weights = jax.nn.softmax(scores, axis=-1).astype(jnp.bfloat16)
    mixture = jnp.einsum(
        "chqk,ckhd->cqhd", weights, value_heads, preferred_element_type=jnp.float32
    ).astype(jnp.bfloat16)
    head_results = mixture.reshape(number, tokens_dev, local_heads * head_size)
    attention = jnp.einsum(
        "itd,de->ite",
        lax.all_to_all(head_results, "node", split_axis=0, concat_axis=2, tiled=True),
        w_output,
        preferred_element_type=jnp.float32,
    )
    middle = inputs + attention
    normed_second = layer_norm(middle).astype(jnp.bfloat16)
    logits = jnp.einsum("itd,de->ite", normed_second, router, preferred_element_type=jnp.float32)
    chosen_mask = routes[..., None] == jnp.arange(num_experts, dtype=jnp.int32)
    chosen_logit = jnp.sum(jnp.where(chosen_mask, logits[:, :, None, :], jnp.float32(0.0)), axis=-1)
    gate_values = jax.nn.sigmoid(chosen_logit)
    flat_routes = routes.reshape(local_images, 2 * tokens_dev)
    slot_index = slot_table(flat_routes, num_experts)
    image_base = jnp.arange(local_images, dtype=jnp.int32)[:, None] * CAP
    position = (flat_routes * slot_count + image_base + slot_index).reshape(-1)
    token_ids = jnp.arange(local_images * 2 * tokens_dev, dtype=jnp.int32) // 2
    source = jnp.full((num_experts * slot_count,), -1, jnp.int32).at[position].set(token_ids)
    token_rows = normed_second.reshape(local_images * tokens_dev, width)
    gathered = jnp.take(token_rows, jnp.maximum(source, 0), axis=0)
    gathered = jnp.where(source[:, None] >= 0, gathered, jnp.zeros_like(gathered))
    outgoing = gathered.reshape(column_count, local_experts, slot_count, width)
    copies = jnp.broadcast_to(outgoing[None], (node_count,) + outgoing.shape)
    copies = copies.reshape(node_count * column_count, local_experts, slot_count, width)
    arrived = lax.all_to_all(copies, ("node", "ep"), split_axis=0, concat_axis=0, tiled=True)
    pre_act = jnp.einsum("lesd,edf->lesf", arrived, w_in, preferred_element_type=jnp.float32)
    hidden = jax.nn.gelu(pre_act, approximate=True).astype(jnp.bfloat16)
    partial_sum = jnp.einsum(
        "lesf,efd->lesd", hidden, w_out, preferred_element_type=jnp.float32
    ).astype(jnp.bfloat16)
    returned = lax.all_to_all(partial_sum, ("node", "ep"), split_axis=0, concat_axis=0, tiled=True)
    returned = returned.astype(jnp.float32).reshape(
        node_count, column_count, local_experts, slot_count, width
    )
    expert_result = jnp.sum(returned, axis=0).astype(jnp.bfloat16)
    result_rows = expert_result.reshape(num_experts * slot_count, width)
    picked = jnp.take(result_rows, position, axis=0).reshape(local_images, tokens_dev, 2, width)
    expert_mix = jnp.sum(gate_values[..., None] * picked.astype(jnp.float32), axis=2)
    return (middle + expert_mix).astype(jnp.bfloat16)


def solution(mesh):
    placed = (
        P(("node", "ep"), None, None),
        P(None, "node"),
        P(None, "node"),
        P(None, "node"),
        P(),
        P(),
        P("ep", None, "node"),
        P("ep", "node", None),
        P(("node", "ep"), None, None),
    )
    return jax.shard_map(
        shards, mesh=mesh, in_specs=placed, out_specs=P(("node", "ep"), None, None), check_vma=False
    )
```

profile of v0, /device:TPU:97, one launch (start us, length us, event | category | flops | bytes accessed | tf_op | source)
XLA Modules:
  0.0 396.5 jit_solution(17544285698891339135)
XLA Ops:
  6.5 1.4 convert_reduce_fusion
  8.0 1.4 fusion.34
  9.4 2.3 fusion.35
  11.7 0.1 copy.100
  11.9 0.1 copy.106
  12.0 0.1 mul.100
  12.2 0.1 eq.54
  12.4 1.5 reduce-window.6
  13.8 0.3 slice_reduce_fusion
  14.3 0.7 reshape.364
  14.9 0.9 fusion.45
  15.9 4.1 %scatter_custom_fusion = s32[768]{0:T(1024)S(1)} fusion(s32[514]{0:T(1024)S(1)} %fusion.49, s32[514]{0:T(1024)S(1)} %add_select_fusion, s32[]{:T(128)} %constant.77.clone.1), kind=kCustom, calls=%fused_computation.80 | custom fusion | bytes 3076 | tf_op jit(solution)/shard_map/scatter | solution.py:74
  20.0 28.8 %all-gather.2.cloned.1.call-done = bf16[4,257,1280]{2,1,0:T(8,128)(2,1)} async-done(((bf16[1,257,1280]{2,1,0:T(8,128)(2,1)}), bf16[4,257,1280]{2,1,0:T(8,128)(2,1)}) %all-gather.2.cloned.1.call-update) | async-done | bytes 2631696 | tf_op jit(solution)/shard_map/all_gather | solution.py:35
  48.8 4.4 %convolution_convert_fusion = bf16[4,257,320]{2,1,0:T(8,128)(2,1)} fusion(bf16[4,257,1280]{2,1,0:T(8,128)(2,1)} %all-gather.2.cloned.1.call-done, bf16[1280,320]{0,1:T(8,128)(2,1)} %param.11), kind=kOutput, calls=%fused_computation.37 | convolution fusion | flops 842466560 | bytes 4108800 | tf_op jit(solution)/shard_map/ctd,de->cte/dot_general | solution.py:40
  53.2 2.3 copy.95
  55.5 4.4 %convolution_convert_fusion.2 = bf16[4,257,320]{2,1,0:T(8,128)(2,1)} fusion(bf16[4,257,1280]{2,1,0:T(8,128)(2,1)} %all-gather.2.cloned.1.call-done, bf16[1280,320]{0,1:T(8,128)(2,1)} %param.12), kind=kOutput, calls=%fused_computation.39 | convolution fusion | flops 842466560 | bytes 4108800 | tf_op jit(solution)/shard_map/ctd,de->cte/dot_general | solution.py:43
  59.9 2.2 copy.93
  62.2 4.4 %convolution_convert_fusion.1 = bf16[4,257,320]{2,1,0:T(8,128)(2,1)} fusion(bf16[4,257,1280]{2,1,0:T(8,128)(2,1)} %all-gather.2.cloned.1.call-done, bf16[1280,320]{0,1:T(8,128)(2,1)} %param.10), kind=kOutput, calls=%fused_computation.38 | convolution fusion | flops 842466560 | bytes 4108800 | tf_op jit(solution)/shard_map/ctd,de->cte/dot_general | solution.py:37
  66.6 2.3 copy.94
  68.9 6.5 %fusion.57 = (f32[4,4,257]{2,1,0:T(4,128)S(1)}, f32[4,4,257,257]{2,3,1,0:T(8,128)}) fusion(bf16[4,257,4,80]{1,3,2,0:T(8,128)(2,1)} %bitcast.114, bf16[4,257,4,80]{1,3,2,0:T(8,128)(2,1)} %bitcast.113), kind=kOutput, calls=%fused_computation.92 | convolution fusion | flops 172256048 | bytes 5559424 | tf_op jit(solution)/shard_map/sub | solution.py:52
  75.4 5.1 %fusion.33 = bf16[4,4,80,257]{3,2,1,0:T(8,128)(2,1)} fusion(bf16[4,257,4,80]{1,3,2,0:T(8,128)(2,1)} %bitcast.112, f32[4,4,257,257]{2,3,1,0:T(8,128)} %get-tuple-element.8, f32[4,4,257]{2,1,0:T(4,128)S(1)} %get-tuple-element.7), kind=kOutput, calls=%fused_computation.36 | convolution fusion | flops 171527968 | bytes 5559424 | tf_op jit(solution)/shard_map/chqk,ckhd->cqhd/dot_general | solution.py:53
  80.5 2.2 copy.97
  82.8 4.4 %all-to-all-start = ((bf16[4,257,320]{2,1,0:T(8,128)(2,1)}), bf16[4,257,320]{2,1,0:T(8,128)(2,1)}, u32[]{:S(2)}, u32[]{:S(2)}) async-start(bf16[4,257,320]{2,1,0:T(8,128)(2,1)} %copy.97), calls=%async_computation | async-start | bytes 1622016 | tf_op jit(solution)/shard_map/all_to_all | solution.py:59
  87.3 0.1 broadcast_in_dim.78
  87.4 11.5 %all-to-all-done = bf16[4,257,320]{2,1,0:T(8,128)(2,1)} async-done(((bf16[4,257,320]{2,1,0:T(8,128)(2,1)}), bf16[4,257,320]{2,1,0:T(8,128)(2,1)}, u32[]{:S(2)}, u32[]{:S(2)}) %all-to-all-start) | async-done | bytes 657952 | tf_op jit(solution)/shard_map/all_to_all | solution.py:59
  98.8 2.3 copy.98
  101.2 2.5 reshape.358
  103.7 3.4 fusion.58
  107.2 0.3 multiply_reduce_fusion.2
  107.5 0.7 copy-done.3
  108.3 1.1 fusion.40
  109.3 6.4 %gather_fusion = bf16[768,1280]{1,0:T(8,128)(2,1)} fusion(bf16[257,1280]{1,0:T(8,128)(2,1)} %fusion.40, s32[1024]{0:T(1024)S(1)} %pad_clamp_fusion.1), kind=kCustom, calls=%fused_computation | custom fusion | bytes 3935232 | tf_op jit(solution)/shard_map/jit(_take)/gather | solution.py:76
  115.7 1.9 select_select_fusion
  117.6 0.5 broadcast_in_dim.83
  118.1 99.0 %all_to_all.25 = bf16[128,1,24,1280]{3,2,1,0:T(8,128)(2,1)} all-to-all(bf16[128,1,24,1280]{3,2,1,0:T(8,128)(2,1)S(1)} %bitcast.110), channel_id=1, replica_groups=mesh['node'=4,'ep'=32] {'node','ep'}, dimensions={0} | all-to-all | bytes 15728640 | tf_op jit(solution)/shard_map/all_to_all | solution.py:81
  217.1 25.9 %convert_bitcast_fusion = bf16[128,1,24,1280]{3,0,2,1:T(8,128)(2,1)} fusion(bf16[1,1280,1280]{2,1,0:T(8,128)(2,1)S(1)} %copy-done, bf16[128,1,24,1280]{3,2,1,0:T(8,128)(2,1)} %all_to_all.25, bf16[1,1280,1280]{2,1,0:T(8,128)(2,1)} %param.15), kind=kOutput, calls=%fused_computation.18 | convolution fusion | flops 20171980800 | bytes 22282240 | tf_op jit(solution)/shard_map/lesf,efd->lesd/dot_general | solution.py:84
  243.0 10.8 %copy.108 = bf16[128,1,24,1280]{3,2,1,0:T(8,128)(2,1)} copy(bf16[128,1,24,1280]{3,0,2,1:T(8,128)(2,1)} %convert_bitcast_fusion) | data formatting | bytes 15728640 | tf_op jit(solution)/shard_map/convert_element_type | solution.py:86
  253.8 10.7 %all-to-all-start.2 = ((bf16[128,1,24,1280]{3,2,1,0:T(8,128)(2,1)}), bf16[128,1,24,1280]{3,2,1,0:T(8,128)(2,1)}, u32[]{:S(2)}, u32[]{:S(2)}) async-start(bf16[128,1,24,1280]{3,2,1,0:T(8,128)(2,1)} %copy.108), calls=%async_computation.2 | async-start | bytes 15728640 | tf_op jit(solution)/shard_map/all_to_all | solution.py:87
  264.5 0.1 reduce_sum.94
  264.7 0.2 copy.105
  264.9 0.3 fusion.60
  265.3 0.1 copy.99
  265.5 97.6 %all-to-all-done.2 = bf16[128,1,24,1280]{3,2,1,0:T(8,128)(2,1)} async-done(((bf16[128,1,24,1280]{3,2,1,0:T(8,128)(2,1)}), bf16[128,1,24,1280]{3,2,1,0:T(8,128)(2,1)}, u32[]{:S(2)}, u32[]{:S(2)}) %all-to-all-start.2) | async-done | bytes 7864352 | tf_op jit(solution)/shard_map/all_to_all | solution.py:87
  363.1 4.3 %bitcast_reduce_fusion = bf16[32,24,1280]{2,1,0:T(8,128)(2,1)S(1)} fusion(bf16[4,32,24,1280]{3,2,1,0:T(8,128)(2,1)} %bitcast.107), kind=kLoop, calls=%fused_computation.13 | loop fusion | flops 2949120 | bytes 9830400 | tf_op jit(solution)/shard_map/reduce_sum | solution.py:91
  367.4 3.5 gather_fusion.1
  370.9 4.1 %gather.15 = bf16[1,257,2,1280]{3,2,1,0:T(2,128)(2,1)} reshape(bf16[514,1280]{1,0:T(8,128)(2,1)} %gather_fusion.1) | data formatting | bytes 2631680 | tf_op jit(solution)/shard_map/jit(_take)/gather | solution.py:93
  375.0 13.6 %multiply_reduce_fusion.1 = f32[257,1280]{1,0:T(8,128)S(1)} fusion(bf16[1,257,2,1280]{3,2,1,0:T(2,128)(2,1)} %gather.15, pred[257,2]{1,0:T(8,128)(4,1)S(1)} %copy.105, f32[257,2]{1,0:T(8,128)S(1)} %copy.99), kind=kLoop, calls=%fused_computation.29 | loop fusion | flops 2302720 | bytes 2634250 | tf_op jit(solution)/shard_map/reduce_sum | solution.py:94
  388.6 1.0 fusion.36
  (39 shorter events, 0.6 us)
Async XLA Ops:
  6.5 210.6 %copy-start = (bf16[1,1280,1280]{2,1,0:T(8,128)(2,1)S(1)}, bf16[1,1280,1280]{2,1,0:T(8,128)(2,1)}, u32[]{:S(2)}) copy-start(bf16[1,1280,1280]{2,1,0:T(8,128)(2,1)} %param.16) | copy-start | bytes 9830404
  6.5 5.2 %copy-start.6 = (s32[1,257,2]{1,2,0:T(2,128)S(1)}, s32[1,257,2]{1,2,0:T(2,128)}, u32[]{:S(2)}) copy-start(s32[1,257,2]{1,2,0:T(2,128)} %param.17) | copy-start | bytes 6172
  6.5 42.2 %all-gather.2.cloned.1.call-start = ((), (), s32[]{:S(2)}) async-start(), calls=%async_computation.3 | async-start | bytes 3379200 | tf_op jit(solution)/shard_map/all_gather | solution.py:35
  82.8 16.1 %all-to-all-start = ((bf16[4,257,320]{2,1,0:T(8,128)(2,1)}), bf16[4,257,320]{2,1,0:T(8,128)(2,1)}, u32[]{:S(2)}, u32[]{:S(2)}) async-start(bf16[4,257,320]{2,1,0:T(8,128)(2,1)} %copy.97), calls=%async_computation | async-start | bytes 1622016 | tf_op jit(solution)/shard_map/all_to_all | solution.py:59
  107.2 1.1 copy-start.3
  253.8 11.2 %copy-start.2 = (bf16[257,1280]{1,0:T(8,128)(2,1)S(1)}, bf16[257,1280]{1,0:T(8,128)(2,1)}, u32[]{:S(2)}) copy-start(bf16[257,1280]{1,0:T(8,128)(2,1)} %fusion.40) | copy-start | bytes 1973764
  253.8 11.2 %copy-start.5 = (bf16[1280,32]{0,1:T(8,128)(2,1)S(1)}, bf16[1280,32]{0,1:T(8,128)(2,1)}, u32[]{:S(2)}) copy-start(bf16[1280,32]{0,1:T(8,128)(2,1)} %param.14) | copy-start | bytes 245764
  253.8 109.4 %all-to-all-start.2 = ((bf16[128,1,24,1280]{3,2,1,0:T(8,128)(2,1)}), bf16[128,1,24,1280]{3,2,1,0:T(8,128)(2,1)}, u32[]{:S(2)}, u32[]{:S(2)}) async-start(bf16[128,1,24,1280]{3,2,1,0:T(8,128)(2,1)} %copy.108), calls=%async_computation.2 | async-start | bytes 15728640 | tf_op jit(solution)/shard_map/all_to_all | solution.py:87
  370.9 18.7 %copy-start.1 = (bf16[1,1280,1280]{2,1,0:T(8,128)(2,1)S(1)}, bf16[1,1280,1280]{2,1,0:T(8,128)(2,1)}, u32[]{:S(2)}) copy-start(bf16[1,1280,1280]{2,1,0:T(8,128)(2,1)} %param.16) | copy-start | bytes 9830404
  375.0 13.6 %copy-start.4 = (f32[1,257,1280]{2,1,0:T(8,128)S(1)}, f32[1,257,1280]{2,1,0:T(8,128)}, u32[]{:S(2)}) copy-start(f32[1,257,1280]{2,1,0:T(8,128)} %copy-done.3) | copy-start | bytes 3947524
Sparse Core Ops, SparseCore 0:
  11.8 36.8 all-gather.1
where the time goes:
time: 397 us; the launch traced here: 396 us
  waiting for transfers between devices  138 us (35%)
  blocking collectives  99 us (25%)
  matrix products  54.6 us (14%)
  local copies, waits for them, and re-layouts  46.4 us (12%)
  other arithmetic  29.8 us (8%)
  starting transfers between devices  15.1 us (4%)
  between operations  13.7 us (3%)
    all_to_all x1, blocking collectives, shards(): lax.all_to_all(copies, ('node', 'ep'), split_axis=0, concat_axis=0, tiled...  99 us
    all_to_all x1, waiting for transfers between devices, shards(): lax.all_to_all(partial_sum, ('node', 'ep'), split_axis=0, concat_axis=0,...  97.6 us
    all_gather x1, waiting for transfers between devices, shards(): shard_rows = lax.all_gather(normed, 'node', axis=0, tiled=True)  28.8 us
    dot_general x1, matrix products, shards(): jnp.einsum('lesf,efd->lesd', hidden, w_out, preferred_element_type=jnp.fl...  25.9 us
    reduce_sum x1, other arithmetic, shards(): jnp.sum(gate_values[..., None] * picked.astype(jnp.float32), axis=2)  13.6 us
    all_to_all x1, waiting for transfers between devices, shards(): lax.all_to_all(head_results, 'node', split_axis=0, concat_axis=2, tiled=T...  11.5 us
    convert_element_type x1, local copies, waits for them, and re-layouts, shards(): partial_sum = jnp.einsum('lesf,efd->lesd', hidden, w_out, preferred_eleme...  10.8 us
    all_to_all x1, starting transfers between devices, shards(): lax.all_to_all(partial_sum, ('node', 'ep'), split_axis=0, concat_axis=0,...  10.7 us
  transfers between devices with their start and end apart: 3, of which 3 were waited for; matrix products, arithmetic and copies ran while one was open for 2% of the time, Pallas kernels for 0%

commit v1 on v0

--- a/solution.py
+++ b/solution.py
@@ -7,6 +7,12 @@
 D = 1280
 HEADS = 16
 CAP = 24
+
+
+def gather_from_all(x, axis, dim):
+    peers = lax.axis_size(axis)
+    repeats = [peers if d == dim else 1 for d in range(x.ndim)]
+    return lax.all_to_all(jnp.tile(x, repeats), axis, split_axis=dim, concat_axis=dim, tiled=True)
 
 
 def layer_norm(values):
@@ -32,7 +38,7 @@
     slot_count = local_images * CAP
     inputs = images.astype(jnp.float32)
     normed = layer_norm(inputs).astype(jnp.bfloat16)
-    shard_rows = lax.all_gather(normed, "node", axis=0, tiled=True)
+    shard_rows = gather_from_all(normed, "node", 0)
     number = shard_rows.shape[0]
     queries = jnp.einsum(
         "ctd,de->cte", shard_rows, w_query, preferred_element_type=jnp.float32

time: 397 us -> 385 us (0.970)
  between operations: 13.7 us -> 0.32 us
  waiting for transfers between devices: 138 us -> 132 us
  starting transfers between devices: 15.1 us -> 19.8 us
    all_gather x1 -> x0, waiting for transfers between devices: 28.8 us -> none  [shards(): shard_rows = lax.all_gather(normed, 'node', axis=0, tiled=True)]
    all_to_all x0 -> x1, waiting for transfers between devices: none -> 24 us  [gather_from_all(): lax.all_to_all(jnp.tile(x, repeats), axis, split_axis=dim, concat_axis=di...]
    all_to_all x0 -> x1, starting transfers between devices: none -> 4.7 us  [gather_from_all(): lax.all_to_all(jnp.tile(x, repeats), axis, split_axis=dim, concat_axis=di...]
where the time goes in v1:
time: 385 us; the launch traced here: 384 us
  waiting for transfers between devices  132 us (34%)
  blocking collectives  99.7 us (26%)
  matrix products  54.6 us (14%)
  local copies, waits for them, and re-layouts  48.1 us (12%)
  other arithmetic  29 us (8%)
  starting transfers between devices  19.8 us (5%)
    all_to_all x1, blocking collectives, shards(): lax.all_to_all(copies, ('node', 'ep'), split_axis=0, concat_axis=0, tiled...  99.7 us
    all_to_all x1, waiting for transfers between devices, shards(): lax.all_to_all(partial_sum, ('node', 'ep'), split_axis=0, concat_axis=0,...  97.6 us
    dot_general x1, matrix products, shards(): jnp.einsum('lesf,efd->lesd', hidden, w_out, preferred_element_type=jnp.fl...  25.9 us
    all_to_all x1, waiting for transfers between devices, gather_from_all(): lax.all_to_all(jnp.tile(x, repeats), axis, split_axis=dim, concat_axis=di...  24 us
    reduce_sum x1, other arithmetic, shards(): jnp.sum(gate_values[..., None] * picked.astype(jnp.float32), axis=2)  13.6 us
    all_to_all x1, waiting for transfers between devices, shards(): lax.all_to_all(head_results, 'node', split_axis=0, concat_axis=2, tiled=T...  10.8 us
    convert_element_type x1, local copies, waits for them, and re-layouts, shards(): partial_sum = jnp.einsum('lesf,efd->lesd', hidden, w_out, preferred_eleme...  10.8 us
    all_to_all x1, starting transfers between devices, shards(): lax.all_to_all(partial_sum, ('node', 'ep'), split_axis=0, concat_axis=0,...  10.7 us
  transfers between devices with their start and end apart: 3, of which 3 were waited for; matrix products, arithmetic and copies ran while one was open for 2% of the time, Pallas kernels for 0%

profile of v1, /device:TPU:97, one launch (start us, length us, event | category | flops | bytes accessed | tf_op | source)
XLA Modules:
  0.0 383.9 jit_solution(10894553052858725679)
XLA Ops:
  0.0 1.4 convert_reduce_fusion
  1.4 1.4 fusion.34
  2.9 1.4 fusion.41
  4.3 1.7 tile.10
  6.0 4.7 %all-to-all-start = ((bf16[4,257,1280]{2,1,0:T(8,128)(2,1)}), bf16[4,257,1280]{2,1,0:T(8,128)(2,1)}, u32[]{:S(2)}, u32[]{:S(2)}) async-start(bf16[4,257,1280]{2,1,0:T(8,128)(2,1)} %tile.10), calls=%async_computation | async-start | bytes 5406720 | tf_op jit(solution)/shard_map/all_to_all | solution.py:15
  10.7 0.1 copy.100
  10.9 0.1 copy.106
  11.0 0.1 mul.100
  11.2 0.1 eq.54
  11.4 1.5 reduce-window.6
  12.8 0.3 slice_reduce_fusion
  13.3 0.7 reshape.367
  14.0 0.9 fusion.46
  14.9 4.1 %scatter_custom_fusion = s32[768]{0:T(1024)S(1)} fusion(s32[514]{0:T(1024)S(1)} %fusion.50, s32[514]{0:T(1024)S(1)} %add_select_fusion, s32[]{:T(128)} %constant.77.clone.1), kind=kCustom, calls=%fused_computation.81 | custom fusion | bytes 3076 | tf_op jit(solution)/shard_map/scatter | solution.py:80
  19.0 24.0 %all-to-all-done = bf16[4,257,1280]{2,1,0:T(8,128)(2,1)} async-done(((bf16[4,257,1280]{2,1,0:T(8,128)(2,1)}), bf16[4,257,1280]{2,1,0:T(8,128)(2,1)}, u32[]{:S(2)}, u32[]{:S(2)}) %all-to-all-start) | async-done | bytes 2631712 | tf_op jit(solution)/shard_map/all_to_all | solution.py:15
  43.0 4.4 %convolution_convert_fusion = bf16[4,257,320]{2,1,0:T(8,128)(2,1)} fusion(bf16[4,257,1280]{2,1,0:T(8,128)(2,1)} %all-to-all-done, bf16[1280,320]{0,1:T(8,128)(2,1)} %param.11), kind=kOutput, calls=%fused_computation.37 | convolution fusion | flops 842466560 | bytes 4108800 | tf_op jit(solution)/shard_map/ctd,de->cte/dot_general | solution.py:46
  47.5 2.3 copy.95
  49.8 4.4 %convolution_convert_fusion.2 = bf16[4,257,320]{2,1,0:T(8,128)(2,1)} fusion(bf16[4,257,1280]{2,1,0:T(8,128)(2,1)} %all-to-all-done, bf16[1280,320]{0,1:T(8,128)(2,1)} %param.12), kind=kOutput, calls=%fused_computation.39 | convolution fusion | flops 842466560 | bytes 4108800 | tf_op jit(solution)/shard_map/ctd,de->cte/dot_general | solution.py:49
  54.2 2.2 copy.93
  56.4 4.4 %convolution_convert_fusion.1 = bf16[4,257,320]{2,1,0:T(8,128)(2,1)} fusion(bf16[4,257,1280]{2,1,0:T(8,128)(2,1)} %all-to-all-done, bf16[1280,320]{0,1:T(8,128)(2,1)} %param.10), kind=kOutput, calls=%fused_computation.38 | convolution fusion | flops 842466560 | bytes 4108800 | tf_op jit(solution)/shard_map/ctd,de->cte/dot_general | solution.py:43
  60.9 2.3 copy.94
  63.2 6.5 %fusion.58 = (f32[4,4,257]{2,1,0:T(4,128)S(1)}, f32[4,4,257,257]{2,3,1,0:T(8,128)}) fusion(bf16[4,257,4,80]{1,3,2,0:T(8,128)(2,1)} %bitcast.116, bf16[4,257,4,80]{1,3,2,0:T(8,128)(2,1)} %bitcast.115), kind=kOutput, calls=%fused_computation.93 | convolution fusion | flops 172256048 | bytes 5559424 | tf_op jit(solution)/shard_map/sub | solution.py:58
  69.7 5.1 %fusion.33 = bf16[4,4,80,257]{3,2,1,0:T(8,128)(2,1)} fusion(bf16[4,257,4,80]{1,3,2,0:T(8,128)(2,1)} %bitcast.114, f32[4,4,257,257]{2,3,1,0:T(8,128)} %get-tuple-element.8, f32[4,4,257]{2,1,0:T(4,128)S(1)} %get-tuple-element.7), kind=kOutput, calls=%fused_computation.36 | convolution fusion | flops 171527968 | bytes 5559424 | tf_op jit(solution)/shard_map/chqk,ckhd->cqhd/dot_general | solution.py:59
  74.8 2.2 copy.97
  77.0 4.4 %all-to-all-start.1 = ((bf16[4,257,320]{2,1,0:T(8,128)(2,1)}), bf16[4,257,320]{2,1,0:T(8,128)(2,1)}, u32[]{:S(2)}, u32[]{:S(2)}) async-start(bf16[4,257,320]{2,1,0:T(8,128)(2,1)} %copy.97), calls=%async_computation.1 | async-start | bytes 1622016 | tf_op jit(solution)/shard_map/all_to_all | solution.py:65
  81.6 10.8 %all-to-all-done.1 = bf16[4,257,320]{2,1,0:T(8,128)(2,1)} async-done(((bf16[4,257,320]{2,1,0:T(8,128)(2,1)}), bf16[4,257,320]{2,1,0:T(8,128)(2,1)}, u32[]{:S(2)}, u32[]{:S(2)}) %all-to-all-start.1) | async-done | bytes 657952 | tf_op jit(solution)/shard_map/all_to_all | solution.py:65
  92.4 2.3 copy.98
  94.7 2.5 reshape.361
  97.3 3.4 fusion.59
  100.8 0.3 multiply_reduce_fusion.2
  101.1 0.7 copy-done.3
  101.8 1.1 fusion.40
  102.9 6.4 %gather_fusion = bf16[768,1280]{1,0:T(8,128)(2,1)} fusion(bf16[257,1280]{1,0:T(8,128)(2,1)} %fusion.40, s32[1024]{0:T(1024)S(1)} %pad_clamp_fusion.1), kind=kCustom, calls=%fused_computation | custom fusion | bytes 3935232 | tf_op jit(solution)/shard_map/jit(_take)/gather | solution.py:82
  109.3 1.9 select_select_fusion
  111.1 0.5 broadcast_in_dim.83
  111.6 99.7 %all_to_all.30 = bf16[128,1,24,1280]{3,2,1,0:T(8,128)(2,1)} all-to-all(bf16[128,1,24,1280]{3,2,1,0:T(8,128)(2,1)S(1)} %bitcast.112), channel_id=1, replica_groups=mesh['node'=4,'ep'=32] {'node','ep'}, dimensions={0} | all-to-all | bytes 15728640 | tf_op jit(solution)/shard_map/all_to_all | solution.py:87
  211.4 25.9 %convert_bitcast_fusion = bf16[128,1,24,1280]{3,0,2,1:T(8,128)(2,1)} fusion(bf16[1,1280,1280]{2,1,0:T(8,128)(2,1)S(1)} %copy-done, bf16[128,1,24,1280]{3,2,1,0:T(8,128)(2,1)} %all_to_all.30, bf16[1,1280,1280]{2,1,0:T(8,128)(2,1)} %param.15), kind=kOutput, calls=%fused_computation.18 | convolution fusion | flops 20171980800 | bytes 22282240 | tf_op jit(solution)/shard_map/lesf,efd->lesd/dot_general | solution.py:90
  237.2 10.8 %copy.108 = bf16[128,1,24,1280]{3,2,1,0:T(8,128)(2,1)} copy(bf16[128,1,24,1280]{3,0,2,1:T(8,128)(2,1)} %convert_bitcast_fusion) | data formatting | bytes 15728640 | tf_op jit(solution)/shard_map/convert_element_type | solution.py:92
  248.0 10.7 %all-to-all-start.3 = ((bf16[128,1,24,1280]{3,2,1,0:T(8,128)(2,1)}), bf16[128,1,24,1280]{3,2,1,0:T(8,128)(2,1)}, u32[]{:S(2)}, u32[]{:S(2)}) async-start(bf16[128,1,24,1280]{3,2,1,0:T(8,128)(2,1)} %copy.108), calls=%async_computation.3 | async-start | bytes 15728640 | tf_op jit(solution)/shard_map/all_to_all | solution.py:93
  259.0 0.2 copy.105
  259.2 0.3 fusion.61
  259.6 0.1 copy.99
  259.7 97.6 %all-to-all-done.3 = bf16[128,1,24,1280]{3,2,1,0:T(8,128)(2,1)} async-done(((bf16[128,1,24,1280]{3,2,1,0:T(8,128)(2,1)}), bf16[128,1,24,1280]{3,2,1,0:T(8,128)(2,1)}, u32[]{:S(2)}, u32[]{:S(2)}) %all-to-all-start.3) | async-done | bytes 7864352 | tf_op jit(solution)/shard_map/all_to_all | solution.py:93
  357.4 4.3 %bitcast_reduce_fusion = bf16[32,24,1280]{2,1,0:T(8,128)(2,1)S(1)} fusion(bf16[4,32,24,1280]{3,2,1,0:T(8,128)(2,1)} %bitcast.109), kind=kLoop, calls=%fused_computation.13 | loop fusion | flops 2949120 | bytes 9830400 | tf_op jit(solution)/shard_map/reduce_sum | solution.py:97
  361.7 3.5 gather_fusion.1
  365.1 4.1 %gather.15 = bf16[1,257,2,1280]{3,2,1,0:T(2,128)(2,1)} reshape(bf16[514,1280]{1,0:T(8,128)(2,1)} %gather_fusion.1) | data formatting | bytes 2631680 | tf_op jit(solution)/shard_map/jit(_take)/gather | solution.py:99
  369.3 13.6 %multiply_reduce_fusion.1 = f32[257,1280]{1,0:T(8,128)S(1)} fusion(bf16[1,257,2,1280]{3,2,1,0:T(2,128)(2,1)} %gather.15, pred[257,2]{1,0:T(8,128)(4,1)S(1)} %copy.105, f32[257,2]{1,0:T(8,128)S(1)} %copy.99), kind=kLoop, calls=%fused_computation.29 | loop fusion | flops 2302720 | bytes 2634250 | tf_op jit(solution)/shard_map/reduce_sum | solution.py:100
  382.9 1.0 fusion.36
  (39 shorter events, 0.8 us)
Async XLA Ops:
  0.0 211.4 %copy-start = (bf16[1,1280,1280]{2,1,0:T(8,128)(2,1)S(1)}, bf16[1,1280,1280]{2,1,0:T(8,128)(2,1)}, u32[]{:S(2)}) copy-start(bf16[1,1280,1280]{2,1,0:T(8,128)(2,1)} %param.16) | copy-start | bytes 9830404
  6.0 4.7 %copy-start.6 = (s32[1,257,2]{1,2,0:T(2,128)S(1)}, s32[1,257,2]{1,2,0:T(2,128)}, u32[]{:S(2)}) copy-start(s32[1,257,2]{1,2,0:T(2,128)} %param.17) | copy-start | bytes 6172
  6.0 37.0 %all-to-all-start = ((bf16[4,257,1280]{2,1,0:T(8,128)(2,1)}), bf16[4,257,1280]{2,1,0:T(8,128)(2,1)}, u32[]{:S(2)}, u32[]{:S(2)}) async-start(bf16[4,257,1280]{2,1,0:T(8,128)(2,1)} %tile.10), calls=%async_computation | async-start | bytes 5406720 | tf_op jit(solution)/shard_map/all_to_all | solution.py:15
  77.0 15.4 %all-to-all-start.1 = ((bf16[4,257,320]{2,1,0:T(8,128)(2,1)}), bf16[4,257,320]{2,1,0:T(8,128)(2,1)}, u32[]{:S(2)}, u32[]{:S(2)}) async-start(bf16[4,257,320]{2,1,0:T(8,128)(2,1)} %copy.97), calls=%async_computation.1 | async-start | bytes 1622016 | tf_op jit(solution)/shard_map/all_to_all | solution.py:65
  100.7 1.1 copy-start.3
  248.0 11.2 %copy-start.2 = (bf16[257,1280]{1,0:T(8,128)(2,1)S(1)}, bf16[257,1280]{1,0:T(8,128)(2,1)}, u32[]{:S(2)}) copy-start(bf16[257,1280]{1,0:T(8,128)(2,1)} %fusion.40) | copy-start | bytes 1973764
  248.0 11.2 %copy-start.5 = (bf16[1280,32]{0,1:T(8,128)(2,1)S(1)}, bf16[1280,32]{0,1:T(8,128)(2,1)}, u32[]{:S(2)}) copy-start(bf16[1280,32]{0,1:T(8,128)(2,1)} %param.14) | copy-start | bytes 245764
  248.0 109.4 %all-to-all-start.3 = ((bf16[128,1,24,1280]{3,2,1,0:T(8,128)(2,1)}), bf16[128,1,24,1280]{3,2,1,0:T(8,128)(2,1)}, u32[]{:S(2)}, u32[]{:S(2)}) async-start(bf16[128,1,24,1280]{3,2,1,0:T(8,128)(2,1)} %copy.108), calls=%async_computation.3 | async-start | bytes 15728640 | tf_op jit(solution)/shard_map/all_to_all | solution.py:93
  365.1 18.7 %copy-start.1 = (bf16[1,1280,1280]{2,1,0:T(8,128)(2,1)S(1)}, bf16[1,1280,1280]{2,1,0:T(8,128)(2,1)}, u32[]{:S(2)}) copy-start(bf16[1,1280,1280]{2,1,0:T(8,128)(2,1)} %param.16) | copy-start | bytes 9830404
  369.2 13.6 %copy-start.4 = (f32[1,257,1280]{2,1,0:T(8,128)S(1)}, f32[1,257,1280]{2,1,0:T(8,128)}, u32[]{:S(2)}) copy-start(f32[1,257,1280]{2,1,0:T(8,128)} %copy-done.3) | copy-start | bytes 3947524
